TPU v7x, 128 devices: a whole 4x4x4 slice. The times are simulated.
128 devices in a mesh: dp: 8 (over z, core), seq: 16 (over y, x).
Axes of the slice: x: 4, y: 4, z: 4, core: 2. Of those that a mesh axis runs over, the one named last changes fastest.
Arguments:
- tokens: bfloat16 [8, 8192, 2048], P('dp', 'seq'), may hold values from -6 to 6
- input_gain: bfloat16 [2048], replicated, may hold values from 0.099609375 to 1.8984375
- qkv_weight: bfloat16 [2048, 6144], P(None, ('dp', 'seq')), may hold values from -0.125 to 0.125
- head_gain: bfloat16 [2048], replicated, may hold values from 0.099609375 to 1.8984375
- prefix_state: float32 [8, 16, 128, 128], P('dp'), may hold values from -256 to 256
Outputs:
- attended: bfloat16 [8, 8192, 2048], P('dp', 'seq')
All inputs are finite; a program needn't handle non-finite values.
Results may differ from a plain program's by a relative error of at most 0.0061.
Values may be sent and summed in bfloat16 or wider, within the bound.
No kernel may reach another device: no remote copies, remote signals or barrier semaphores. Data moves between devices by JAX's collectives and lax.ppermute only.
A program may use at most 128 MiB of HBM per device.

v0:
```python
import jax
import jax.numpy as jnp
from jax import lax
from jax.sharding import Mesh, PartitionSpec as P

D = 2048
H = 16
DH = 128
BLOCK = 512
epsilon = 1e-05


def feature_map(inputs):
    return jnp.where(inputs > 0, inputs + 1.0, jnp.exp(jnp.minimum(inputs, 0.0)))


def body(tokens, input_gain, qkv_weight, head_gain, prefix_state):
    inputs = tokens[0].astype(jnp.float32)
    normed = inputs * lax.rsqrt(jnp.mean(inputs * inputs, axis=-1, keepdims=True) + epsilon)
    normed = (normed * input_gain.astype(jnp.float32)).astype(jnp.bfloat16)
    tok_rows = normed.shape[0]
    weight = lax.all_gather(qkv_weight, ("dp", "y", "x"), axis=1, tiled=True)
    keys_t = lax.dot_general(
        weight[:, D : 2 * D], normed, (((0,), (1,)), ((), ())), preferred_element_type=jnp.float32
    )
    keys_t = feature_map(keys_t).astype(jnp.bfloat16).reshape(H, DH, tok_rows)
    values = jnp.dot(normed, weight[:, 2 * D :], preferred_element_type=jnp.float32)
    values = values.astype(jnp.bfloat16).reshape(tok_rows, H, DH)
    local = jnp.einsum("hdt,the->hde", keys_t, values, preferred_element_type=jnp.float32).astype(
        jnp.bfloat16
    )
    gathered = lax.all_gather(local[None], ("y", "x"), axis=0, tiled=True)
    seq_here = lax.axis_index(("y", "x"))
    earlier = (jnp.arange(gathered.shape[0]) < seq_here).astype(jnp.bfloat16)
    before = jnp.einsum("c,chde->hde", earlier, gathered, preferred_element_type=jnp.float32)
    memory = prefix_state[0] + before
    queries = jnp.dot(normed, weight[:, :D], preferred_element_type=jnp.float32)
    queries = feature_map(queries).astype(jnp.bfloat16).reshape(tok_rows, H, DH)
    causal = jnp.arange(tok_rows)[:, None] >= jnp.arange(tok_rows)[None, :]
    gains = head_gain.astype(jnp.float32).reshape(H, DH)
    scores = jnp.einsum("bhd,hdc->hbc", queries, keys_t, preferred_element_type=jnp.float32)
    scores = jnp.where(causal[None], scores, 0.0).astype(jnp.bfloat16)
    within = jnp.einsum("hbc,che->bhe", scores, values, preferred_element_type=jnp.float32)
    carried = jnp.einsum(
        "bhd,hde->bhe", queries, memory.astype(jnp.bfloat16), preferred_element_type=jnp.float32
    )
    numerator = carried + within
    scale = lax.rsqrt(jnp.mean(numerator * numerator, axis=-1, keepdims=True) + epsilon)
    attended = (numerator * scale * gains).astype(jnp.bfloat16)
    return attended.reshape(1, tok_rows, H * DH)


def solution(mesh):
    n_dp, n_seq = mesh.devices.shape
    n_x = int(round(n_seq**0.5))
    split = Mesh(mesh.devices.reshape(n_dp, n_seq // n_x, n_x), ("dp", "y", "x"))
    cols = ("y", "x")
    placed = (P("dp", cols, None), P(), P(None, ("dp", "y", "x")), P(), P("dp", None, None, None))
    return jax.shard_map(
        body, mesh=split, in_specs=placed, out_specs=P("dp", cols, None), check_vma=False
    )
```

profile of v0, /device:TPU:1, one launch (start us, length us, event | category | flops | bytes accessed | tf_op | source)
XLA Modules:
  0.0 226.6 jit_solution(10848702317231720216)
XLA Ops:
  6.5 0.0 all-gather.4.cloned.1.call-start
  6.5 0.7 all-gather.4.cloned.1.call-update
  7.3 0.0 all-gather.6.cloned.1.call-start
  7.3 0.7 convert_element_type.40
  8.0 2.1 fusion.8
  10.1 97.0 %all-gather.4.cloned.1.call-done = bf16[2048,6144]{0,1:T(8,128)(2,1)} async-done(((bf16[2048,48]{0,1:T(8,128)(2,1)}), bf16[2048,6144]{0,1:T(8,128)(2,1)}) %all-gather.4.cloned.1.call-update) | async-done | bytes 25165840 | tf_op jit(solution)/shard_map/all_gather | solution.py:22
  107.1 9.9 %fusion.14 = bf16[512,2048]{1,0:T(8,128)(2,1)} fusion(bf16[2048,6144]{0,1:T(8,128)(2,1)} %all-gather.4.cloned.1.call-done, bf16[1,512,2048]{2,1,0:T(8,128)(2,1)} %param.5, f32[2048]{0:T(1024)S(1)} %convert_element_type.40, f32[512]{0:T(512)S(1)} %add_rsqrt_fusion.1), kind=kOutput, calls=%fused_computation.21 | convolution fusion | flops 4300210176 | bytes 12593152 | tf_op jit(solution)/shard_map/dot_general | solution.py:27
  117.0 2.9 %copy.23 = bf16[512,2048]{0,1:T(8,128)(2,1)S(1)} copy(bf16[512,2048]{1,0:T(8,128)(2,1)} %fusion.14) | data formatting | bytes 4194304 | tf_op jit(solution)/shard_map/reshape | solution.py:28
  119.9 10.3 %fusion.21 = bf16[2048,512]{0,1:T(8,128)(2,1)} fusion(bf16[2048,6144]{0,1:T(8,128)(2,1)} %all-gather.4.cloned.1.call-done, bf16[1,512,2048]{2,1,0:T(8,128)(2,1)} %param.5, f32[2048]{0:T(1024)S(1)} %convert_element_type.40, f32[512]{0:T(512)S(1)} %add_rsqrt_fusion.1), kind=kOutput, calls=%fused_computation.22 | convolution fusion | flops 4304404480 | bytes 12593152 | tf_op jit(solution)/shard_map/dot_general | solution.py:23
  130.1 0.0 copy-start.3
  130.1 3.9 %copy.22 = bf16[2048,512]{1,0:T(8,128)(2,1)} copy(bf16[2048,512]{0,1:T(8,128)(2,1)} %fusion.21) | data formatting | bytes 4194304 | tf_op jit(solution)/shard_map/reshape | solution.py:26
  134.1 3.1 %convolution_convert_fusion = bf16[16,128,128]{2,1,0:T(8,128)(2,1)} fusion(bf16[16,128,512]{2,1,0:T(8,128)(2,1)} %bitcast.56, bf16[512,16,128]{0,2,1:T(8,128)(2,1)S(1)} %bitcast.54), kind=kOutput, calls=%fused_computation.30 | convolution fusion | flops 268697600 | bytes 4718592 | tf_op jit(solution)/shard_map/hdt,the->hde/dot_general | solution.py:29
  137.2 0.0 all-gather.6.cloned.1.call-update
  137.2 0.1 iota_compare_fusion
  137.3 0.0 copy-done.3
  137.3 10.4 %fusion.31 = bf16[64,16,8,128]{3,2,1,0:T(8,128)(2,1)} fusion(bf16[2048,6144]{0,1:T(8,128)(2,1)} %all-gather.4.cloned.1.call-done, bf16[1,512,2048]{2,1,0:T(8,128)(2,1)} %param.5, f32[2048]{0:T(1024)S(1)} %convert_element_type.40, f32[512]{0:T(512)S(1)} %add_rsqrt_fusion.1), kind=kOutput, calls=%fused_computation.29 | convolution fusion | flops 4304404480 | bytes 12593152 | tf_op jit(solution)/shard_map/dot_general | solution.py:37
  147.7 9.2 %fusion.24 = f32[16,128,512]{2,1,0:T(8,128)} fusion(bf16[512,16,128]{0,2,1:T(8,128)(2,1)S(1)} %bitcast.55, bf16[16,128,512]{2,1,0:T(8,128)(2,1)} %bitcast.57, pred[512,512]{1,0:T(8,128)(4,1)S(1)} %iota_compare_fusion, bf16[64,16,8,128]{3,2,1,0:T(8,128)(2,1)} %fusion.31), kind=kOutput, calls=%fused_computation.23 | convolution fusion | flops 2155872256 | bytes 10747904 | tf_op jit(solution)/shard_map/hbc,che->bhe/dot_general | solution.py:43
  156.8 50.2 %all-gather.6.cloned.1.call-done = bf16[256,128,128]{2,1,0:T(8,128)(2,1)} async-done(((bf16[16,128,128]{2,1,0:T(8,128)(2,1)}), bf16[256,128,128]{2,1,0:T(8,128)(2,1)}) %all-gather.6.cloned.1.call-update) | async-done | bytes 8388624 | tf_op jit(solution)/shard_map/all_gather | solution.py:32
  207.0 0.0 copy-start
  207.0 0.0 copy-start.1
  207.0 0.0 copy-start.2
  207.0 8.7 %fusion.6 = f32[1,16,128,128]{3,0,2,1:T(1,128)S(1)} fusion(bf16[16,16,128,128]{3,2,1,0:T(8,128)(2,1)} %bitcast.53, s32[]{:T(128)S(6)} %add.45), kind=kOutput, calls=%fused_computation.7 | convolution fusion | flops 8388624 | bytes 9437188 | tf_op jit(solution)/shard_map/c,chde->hde/dot_general | solution.py:35
  215.7 0.0 copy-done
  215.7 0.0 copy-done.1
  215.7 0.0 copy-done.2
  215.7 1.0 fusion.11
  216.8 0.6 fusion.13
  217.4 2.4 %copy.17 = bf16[1,512,2048]{2,1,0:T(8,128)(2,1)} copy(bf16[1,512,2048]{1,2,0:T(8,128)(2,1)S(1)} %bitcast.58) | data formatting | bytes 4194304 | tf_op jit(solution)/shard_map/reshape | solution.py:50
  (3 shorter events, 0.0 us)
Async XLA Ops:
  6.5 100.6 %all-gather.4.cloned.1.call-start = ((), (), s32[]{:S(2)}) async-start(), calls=%async_computation | async-start | bytes 25362432 | tf_op jit(solution)/shard_map/all_gather | solution.py:22
  7.3 199.8 %all-gather.6.cloned.1.call-start = ((), (), s32[]{:S(2)}) async-start(), calls=%async_computation.1 | async-start | bytes 8912896 | tf_op jit(solution)/shard_map/all_gather | solution.py:32
  130.1 7.2 %copy-start.3 = (bf16[2048]{0:T(1024)(128)(2,1)S(1)}, bf16[2048]{0:T(1024)(128)(2,1)}, u32[]{:S(2)}) copy-start(bf16[2048]{0:T(1024)(128)(2,1)} %param.8) | copy-start | bytes 12292
  207.0 8.7 %copy-start = (f32[16,128,512]{2,1,0:T(8,128)S(1)}, f32[16,128,512]{2,1,0:T(8,128)}, u32[]{:S(2)}) copy-start(f32[16,128,512]{2,1,0:T(8,128)} %fusion.24) | copy-start | bytes 12582916
  207.0 8.7 %copy-start.1 = (bf16[64,16,8,128]{3,2,1,0:T(8,128)(2,1)S(1)}, bf16[64,16,8,128]{3,2,1,0:T(8,128)(2,1)}, u32[]{:S(2)}) copy-start(bf16[64,16,8,128]{3,2,1,0:T(8,128)(2,1)} %fusion.31) | copy-start | bytes 6291460
  207.0 8.7 %copy-start.2 = (f32[1,16,128,128]{3,2,1,0:T(8,128)S(1)}, f32[1,16,128,128]{3,2,1,0:T(8,128)}, u32[]{:S(2)}) copy-start(f32[1,16,128,128]{3,2,1,0:T(8,128)} %param.9) | copy-start | bytes 3145732
Sparse Core Ops, SparseCore 0:
  10.4 96.6 all-gather.3
  137.3 69.6 all-gather.5
where the time goes:
time: 227 us
  waiting for transfers between devices  148 us (65%)
  matrix products  52.5 us (23%)
  between operations  13.5 us (6%)
  local copies, waits for them, and re-layouts  9.18 us (4%)
  other arithmetic  3.51 us (2%)
    all_gather x1, waiting for transfers between devices, body(): weight = lax.all_gather(qkv_weight, ('dp', 'y', 'x'), axis=1, tiled=True)  97 us
    all_gather x1, waiting for transfers between devices, body(): gathered = lax.all_gather(local[None], ('y', 'x'), axis=0, tiled=True)  50.2 us
    dot_general x1, matrix products, body(): queries = jnp.dot(normed, weight[:, :D], preferred_element_type=jnp.float32)  10.4 us
    dot_general x1, matrix products, body(): lax.dot_general(weight[:, D:2 * D], normed, (((0,), (1,)), ((), ())), pre...  10.3 us
    dot_general x1, matrix products, body(): jnp.dot(normed, weight[:, 2 * D:], preferred_element_type=jnp.float32)  9.89 us
    dot_general x1, matrix products, body(): jnp.einsum('hbc,che->bhe', scores, values, preferred_element_type=jnp.flo...  9.16 us
    dot_general x1, matrix products, body(): jnp.einsum('c,chde->hde', earlier, gathered, preferred_element_type=jnp.f...  8.66 us
  transfers between devices with their start and end apart: 2, of which 2 were waited for; matrix products, arithmetic and copies ran while one was open for 10% of the time, Pallas kernels for 0%

commit v1 on v0

--- a/solution.py
+++ b/solution.py
@@ -19,7 +19,12 @@
     normed = inputs * lax.rsqrt(jnp.mean(inputs * inputs, axis=-1, keepdims=True) + epsilon)
     normed = (normed * input_gain.astype(jnp.float32)).astype(jnp.bfloat16)
     tok_rows = normed.shape[0]
-    weight = lax.all_gather(qkv_weight, ("dp", "y", "x"), axis=1, tiled=True)
+    weight = jnp.concatenate(
+        lax.all_to_all(
+            jnp.stack([qkv_weight] * lax.axis_size(("dp", "y", "x"))), ("dp", "y", "x"), 0, 0
+        ),
+        axis=1,
+    )
     keys_t = lax.dot_general(
         weight[:, D : 2 * D], normed, (((0,), (1,)), ((), ())), preferred_element_type=jnp.float32
     )

time: 227 us -> 556 us (2.45)
  waiting for transfers between devices: 148 us -> 459 us
  starting transfers between devices: 0.04 us -> 11.9 us
  local copies, waits for them, and re-layouts: 9.18 us -> 18.5 us
    all_to_all x0 -> x1, waiting for transfers between devices: none -> 376 us  [body(): lax.all_to_all(jnp.stack([qkv_weight] * lax.axis_size(('dp', 'y', 'x'))),...]
    all_gather x1 -> x0, waiting for transfers between devices: 97 us -> none  [body(): weight = lax.all_gather(qkv_weight, ('dp', 'y', 'x'), axis=1, tiled=True)]
    all_gather x1, waiting for transfers between devices: 50.2 us -> 83.4 us  [body(): gathered = lax.all_gather(local[None], ('y', 'x'), axis=0, tiled=True)]
    all_to_all x0 -> x1, starting transfers between devices: none -> 11.9 us  [body(): lax.all_to_all(jnp.stack([qkv_weight] * lax.axis_size(('dp', 'y', 'x'))),...]
    another operation x0 -> x1, local copies, waits for them, and re-layouts: none -> 9.34 us  [body(): jnp.stack([qkv_weight] * lax.axis_size(('dp', 'y', 'x')))]
  transfers between devices with their start and end apart: 2 -> 2, of which waited for: 2 -> 2; matrix products, arithmetic and copies ran while one was open for 10% -> 4% of each run, Pallas kernels for 0% -> 0%
where the time goes in v1:
time: 556 us
  waiting for transfers between devices  459 us (83%)
  matrix products  51.2 us (9%)
  local copies, waits for them, and re-layouts  18.5 us (3%)
  between operations  13.5 us (2%)
  starting transfers between devices  11.9 us (2%)
    all_to_all x1, waiting for transfers between devices, body(): lax.all_to_all(jnp.stack([qkv_weight] * lax.axis_size(('dp', 'y', 'x'))),...  376 us
    all_gather x1, waiting for transfers between devices, body(): gathered = lax.all_gather(local[None], ('y', 'x'), axis=0, tiled=True)  83.4 us
    all_to_all x1, starting transfers between devices, body(): lax.all_to_all(jnp.stack([qkv_weight] * lax.axis_size(('dp', 'y', 'x'))),...  11.9 us
  transfers between devices with their start and end apart: 2, of which 2 were waited for; matrix products, arithmetic and copies ran while one was open for 4% of the time, Pallas kernels for 0%

profile of v1, /device:TPU:1, one launch (start us, length us, event | category | flops | bytes accessed | tf_op | source)
XLA Modules:
  0.0 555.6 jit_solution(6321737969137162657)
XLA Ops:
  6.5 9.3 %stack.2 = bf16[128,2048,48]{1,2,0:T(8,128)(2,1)} broadcast(bf16[2048,48]{0,1:T(8,128)(2,1)} %param.7), dimensions={1,2} | broadcast | bytes 25362432 | tf_op jit(solution)/shard_map/stack | solution.py:24
  15.9 0.0 copy-start.4
  15.9 0.0 copy-start.1
  15.9 11.9 %all-to-all-start = ((bf16[128,2048,48]{1,2,0:T(8,128)(2,1)}), bf16[128,2048,48]{1,2,0:T(8,128)(2,1)}, u32[]{:S(2)}, u32[]{:S(2)}) async-start(bf16[128,2048,48]{1,2,0:T(8,128)(2,1)} %stack.2), calls=%async_computation | async-start | bytes 50331648 | tf_op jit(solution)/shard_map/all_to_all | solution.py:23
  27.8 0.0 all-gather.3.cloned.1.call-start
  27.8 0.0 copy-done.4
  27.9 0.0 copy-done.1
  27.9 0.5 fusion.8
  28.4 375.7 %all-to-all-done = bf16[128,2048,48]{1,2,0:T(8,128)(2,1)} async-done(((bf16[128,2048,48]{1,2,0:T(8,128)(2,1)}), bf16[128,2048,48]{1,2,0:T(8,128)(2,1)}, u32[]{:S(2)}, u32[]{:S(2)}) %all-to-all-start) | async-done | bytes 25165856 | tf_op jit(solution)/shard_map/all_to_all | solution.py:23
  404.0 9.7 %fusion.21 = bf16[2048,512]{0,1:T(8,128)(2,1)} fusion(bf16[2048,6144]{0,1:T(8,128)(2,1)} %bitcast.6, bf16[1,512,2048]{2,1,0:T(8,128)(2,1)S(1)} %copy-done.1, f32[2048]{0:T(1024)S(1)} %convert_element_type.40, f32[512]{0:T(512)S(1)} %add_rsqrt_fusion.1), kind=kOutput, calls=%fused_computation.22 | convolution fusion | flops 4304404480 | bytes 12593152 | tf_op jit(solution)/shard_map/dot_general | solution.py:28
  413.7 9.2 %fusion.14 = bf16[512,2048]{1,0:T(8,128)(2,1)} fusion(bf16[2048,6144]{0,1:T(8,128)(2,1)} %bitcast.6, bf16[1,512,2048]{2,1,0:T(8,128)(2,1)S(1)} %copy-done.1, f32[2048]{0:T(1024)S(1)} %convert_element_type.40, f32[512]{0:T(512)S(1)} %add_rsqrt_fusion.1), kind=kOutput, calls=%fused_computation.21 | convolution fusion | flops 4300210176 | bytes 12593152 | tf_op jit(solution)/shard_map/dot_general | solution.py:32
  422.9 2.9 copy.31
  425.8 0.0 copy-start.5
  425.8 3.9 copy.32
  429.7 3.1 convolution_convert_fusion
  432.8 0.0 all-gather.3.cloned.1.call-update
  432.8 0.1 iota_compare_fusion
  432.9 0.0 copy-done.5
  432.9 10.4 %fusion.31 = bf16[64,16,8,128]{3,2,1,0:T(8,128)(2,1)} fusion(bf16[2048,6144]{0,1:T(8,128)(2,1)} %bitcast.6, bf16[1,512,2048]{2,1,0:T(8,128)(2,1)} %param.5, f32[2048]{0:T(1024)S(1)} %convert_element_type.40, f32[512]{0:T(512)S(1)} %add_rsqrt_fusion.1), kind=kOutput, calls=%fused_computation.29 | convolution fusion | flops 4304404480 | bytes 12593152 | tf_op jit(solution)/shard_map/dot_general | solution.py:42
  443.3 9.2 %fusion.24 = f32[16,128,512]{2,1,0:T(8,128)} fusion(bf16[512,16,128]{0,2,1:T(8,128)(2,1)} %bitcast.60, bf16[16,128,512]{2,1,0:T(8,128)(2,1)S(1)} %bitcast.58, pred[512,512]{1,0:T(8,128)(4,1)S(1)} %iota_compare_fusion, bf16[64,16,8,128]{3,2,1,0:T(8,128)(2,1)} %fusion.31), kind=kOutput, calls=%fused_computation.23 | convolution fusion | flops 2155872256 | bytes 10747904 | tf_op jit(solution)/shard_map/hbc,che->bhe/dot_general | solution.py:48
  452.5 83.4 %all-gather.3.cloned.1.call-done = bf16[256,128,128]{2,1,0:T(8,128)(2,1)} async-done(((bf16[16,128,128]{2,1,0:T(8,128)(2,1)}), bf16[256,128,128]{2,1,0:T(8,128)(2,1)}) %all-gather.3.cloned.1.call-update) | async-done | bytes 8388624 | tf_op jit(solution)/shard_map/all_gather | solution.py:37
  536.0 0.0 copy-start
  536.0 0.0 copy-start.2
  536.0 0.0 copy-start.3
  536.0 8.7 %fusion.6 = f32[1,16,128,128]{3,0,2,1:T(1,128)S(1)} fusion(bf16[16,16,128,128]{3,2,1,0:T(8,128)(2,1)} %bitcast.56, s32[]{:T(128)S(6)} %add.45), kind=kOutput, calls=%fused_computation.7 | convolution fusion | flops 8388624 | bytes 9437188 | tf_op jit(solution)/shard_map/c,chde->hde/dot_general | solution.py:40
  544.6 0.0 copy-done
  544.6 0.0 copy-done.2
  544.6 0.0 copy-done.3
  544.7 1.0 fusion.11
  545.7 0.6 fusion.13
  546.3 2.4 copy.26
  (4 shorter events, 0.0 us)
Async XLA Ops:
  15.9 12.0 %copy-start.4 = (bf16[2048]{0:T(1024)(128)(2,1)S(1)}, bf16[2048]{0:T(1024)(128)(2,1)}, u32[]{:S(2)}) copy-start(bf16[2048]{0:T(1024)(128)(2,1)} %param.6) | copy-start | bytes 12292
  15.9 12.0 %copy-start.1 = (bf16[1,512,2048]{2,1,0:T(8,128)(2,1)S(1)}, bf16[1,512,2048]{2,1,0:T(8,128)(2,1)}, u32[]{:S(2)}) copy-start(bf16[1,512,2048]{2,1,0:T(8,128)(2,1)} %param.5) | copy-start | bytes 6291460
  15.9 388.1 %all-to-all-start = ((bf16[128,2048,48]{1,2,0:T(8,128)(2,1)}), bf16[128,2048,48]{1,2,0:T(8,128)(2,1)}, u32[]{:S(2)}, u32[]{:S(2)}) async-start(bf16[128,2048,48]{1,2,0:T(8,128)(2,1)} %stack.2), calls=%async_computation | async-start | bytes 50331648 | tf_op jit(solution)/shard_map/all_to_all | solution.py:23
  27.8 508.2 %all-gather.3.cloned.1.call-start = ((), (), s32[]{:S(2)}) async-start(), calls=%async_computation.1 | async-start | bytes 8912896 | tf_op jit(solution)/shard_map/all_gather | solution.py:37
  425.8 7.2 %copy-start.5 = (bf16[2048]{0:T(1024)(128)(2,1)S(1)}, bf16[2048]{0:T(1024)(128)(2,1)}, u32[]{:S(2)}) copy-start(bf16[2048]{0:T(1024)(128)(2,1)} %param.8) | copy-start | bytes 12292
  536.0 8.7 %copy-start = (f32[16,128,512]{2,1,0:T(8,128)S(1)}, f32[16,128,512]{2,1,0:T(8,128)}, u32[]{:S(2)}) copy-start(f32[16,128,512]{2,1,0:T(8,128)} %fusion.24) | copy-start | bytes 12582916
  536.0 8.7 %copy-start.2 = (bf16[64,16,8,128]{3,2,1,0:T(8,128)(2,1)S(1)}, bf16[64,16,8,128]{3,2,1,0:T(8,128)(2,1)}, u32[]{:S(2)}) copy-start(bf16[64,16,8,128]{3,2,1,0:T(8,128)(2,1)} %fusion.31) | copy-start | bytes 6291460
  536.0 8.7 %copy-start.3 = (f32[1,16,128,128]{3,2,1,0:T(8,128)S(1)}, f32[1,16,128,128]{3,2,1,0:T(8,128)}, u32[]{:S(2)}) copy-start(f32[1,16,128,128]{3,2,1,0:T(8,128)} %param.9) | copy-start | bytes 3145732
Sparse Core Ops, SparseCore 0:
  433.0 102.9 all-gather.2
